TPU v7x, 256 devices: a whole 4x4x8 slice. The times are simulated.
256 devices in a mesh: seq: 32 (over z, y_lo, core), head: 8 (over x, y_hi).
Axes of the slice: x: 4, y: 4 (y_hi: 2, y_lo: 2; y = y_hi * 2 + y_lo), z: 8, core: 2. Of those that a mesh axis runs over, the one named last changes fastest.
Arguments:
- queries: bfloat16 [32768, 1024], P('seq', 'head'), may hold values from -6 to 6
- keys: bfloat16 [32768, 1024], P('seq', 'head'), may hold values from -6 to 6
- values: bfloat16 [32768, 1024], P('seq', 'head'), may hold values from -6 to 6
- gates: bfloat16 [32768, 1024], P('seq', 'head'), may hold values from -6 to 6
- sessions: int32 [32768], P('seq'), may hold values from 0 to 15, never falling along the last dimension, each value on 1 to 3072 neighbouring positions
- score_bias: float32 [8], P('head'), may hold values from -1 to 1
- grad_out: bfloat16 [32768, 1024], P('seq', 'head'), may hold values from -6 to 6
- w_out: bfloat16 [1024, 1024], P('head'), may hold values from -0.1875 to 0.1875
Outputs:
- grad_queries: float32 [32768, 1024], P('seq', 'head')
- grad_keys: float32 [32768, 1024], P('seq', 'head')
- grad_values: float32 [32768, 1024], P('seq', 'head')
- grad_gates: float32 [32768, 1024], P('seq', 'head')
- grad_w_out: float32 [1024, 1024], P('head', 'seq')
Inputs may be any that keep to these rules, and one draw needn't show every extreme that they name: `sessions`: session numbers never fall from one event to the next; every session number is used, each session has 1 to 3072 events and one has exactly 3072.
All inputs are finite; a program needn't handle non-finite values.
Results may differ from a plain program's by a relative error of at most 0.0042.
Values may be sent and summed in bfloat16 or wider, within the bound.
No kernel may reach another device: no remote copies, remote signals or barrier semaphores. Data moves between devices by JAX's collectives and lax.ppermute only.
A program may use at most 128 MiB of HBM per device.

v0:
```python
import math
import jax
import jax.numpy as jnp
from jax import lax
from jax.sharding import PartitionSpec as P

DH = 128
back_steps = (1, 2, 3)
norm_eps = 1e-05


def shifted(block, axis, distance):
    devices = range(lax.axis_size(axis))
    route = [(i - distance, i) for i in devices if i - distance in devices]
    return lax.ppermute(block, axis, route)


def silu_parts(scores):
    sigma = jax.nn.sigmoid(scores)
    return (scores * sigma, sigma * (1.0 + scores * (1.0 - sigma)))


def per_device(queries, keys, values, gates, sessions, score_bias, grad_out, w_out):
    row_count = queries.shape[0]
    feature_count = queries.shape[1]
    head_count = feature_count // DH
    scale = 1.0 / math.sqrt(DH)
    my_index = lax.axis_index("seq")
    q_heads = queries.reshape(row_count, head_count, DH)
    bias_col = score_bias.reshape(head_count, 1, 1)
    offsets = jnp.arange(row_count, dtype=jnp.int32)
    packed = jnp.stack([keys, values])
    windows = [(packed, sessions)]
    for distance in back_steps:
        windows.append(shifted((packed, sessions), "seq", distance))
    prepared = []
    for distance in range(4):
        key_pack, key_sessions = windows[distance]
        allowed = (sessions[:, None] == key_sessions[None, :]) & (my_index >= distance)
        if distance == 0:
            allowed = allowed & (offsets[None, :] <= offsets[:, None])
        k_heads = key_pack[0].reshape(row_count, head_count, DH)
        v_heads = key_pack[1].reshape(row_count, head_count, DH)
        prepared.append((k_heads, v_heads, allowed))

    def pair_scores(query_heads, k_heads):
        raw = jnp.einsum("ihd,jhd->hij", query_heads, k_heads, preferred_element_type=jnp.float32)
        return raw * scale + bias_col

    attended = jnp.zeros((row_count, head_count, DH), jnp.float32)
    for k_heads, v_heads, allowed in prepared:
        act, deriv = silu_parts(pair_scores(q_heads, k_heads))
        weights = jnp.where(allowed[None], act, 0.0).astype(jnp.bfloat16)
        attended = attended + jnp.einsum(
            "hij,jhd->ihd", weights, v_heads, preferred_element_type=jnp.float32
        )
    centered = attended - jnp.mean(attended, axis=-1, keepdims=True)
    inv_std = lax.rsqrt(jnp.mean(centered * centered, axis=-1, keepdims=True) + norm_eps)
    normed = centered * inv_std
    gate_heads = gates.reshape(row_count, head_count, DH).astype(jnp.float32)
    mixed = (normed * gate_heads).astype(jnp.bfloat16).reshape(row_count, feature_count)
    column_block = lax.all_gather(grad_out, "head", axis=1, tiled=True)
    grad_mixed = lax.dot_general(
        column_block, w_out, (((1,), (1,)), ((), ())), preferred_element_type=jnp.float32
    )
    product = lax.dot_general(
        mixed, column_block, (((0,), (0,)), ((), ())), preferred_element_type=jnp.float32
    )
    weight_rows = product
    grad_mixed, weight_rows = (grad_mixed, weight_rows)
    grad_w_out = lax.psum_scatter(weight_rows, "seq", scatter_dimension=1, tiled=True)
    grad_mixed = grad_mixed.reshape(row_count, head_count, DH)
    grad_gates = (grad_mixed * normed).reshape(row_count, feature_count)
    grad_normed = grad_mixed * gate_heads
    grad_attended = (
        grad_normed
        - jnp.mean(grad_normed, axis=-1, keepdims=True)
        - normed * jnp.mean(grad_normed * normed, axis=-1, keepdims=True)
    ) * inv_std
    grad_attended = grad_attended.astype(jnp.bfloat16)
    grad_queries = jnp.zeros((row_count, head_count, DH), jnp.float32)
    key_terms = []
    for window_index in range(4):
        k_heads, v_heads, allowed = prepared[window_index]
        scores = pair_scores(q_heads, k_heads)
        key_act, key_deriv = silu_parts(scores)
        key_weights = jnp.where(allowed[None], key_act, 0.0).astype(jnp.bfloat16)
        values_term = jnp.einsum(
            "hij,ihd->jhd", key_weights, grad_attended, preferred_element_type=jnp.float32
        )
        grad_weights = jnp.einsum(
            "ihd,jhd->hij", grad_attended, v_heads, preferred_element_type=jnp.float32
        )
        grad_scores = jnp.where(allowed[None], grad_weights * key_deriv * scale, 0.0).astype(
            jnp.bfloat16
        )
        keys_term = jnp.einsum(
            "hij,ihd->jhd", grad_scores, q_heads, preferred_element_type=jnp.float32
        )
        grad_scores, term_pair = (
            grad_scores,
            jnp.stack(
                [
                    keys_term.reshape(row_count, feature_count),
                    values_term.reshape(row_count, feature_count),
                ]
            ),
        )
        key_terms.append(term_pair)
        grad_queries = grad_queries + jnp.einsum(
            "hij,jhd->ihd", grad_scores, k_heads, preferred_element_type=jnp.float32
        )
    summed = key_terms[0]
    for distance in back_steps:
        summed = summed + shifted(key_terms[distance], "seq", -distance)
    return (
        grad_queries.reshape(row_count, feature_count),
        summed[0],
        summed[1],
        grad_gates,
        grad_w_out,
    )


def solution(mesh):
    return jax.shard_map(
        per_device,
        mesh=mesh,
        in_specs=(
            P("seq", "head"),
            P("seq", "head"),
            P("seq", "head"),
            P("seq", "head"),
            P("seq"),
            P("head"),
            P("seq", "head"),
            P("head", None),
        ),
        out_specs=(
            P("seq", "head"),
            P("seq", "head"),
            P("seq", "head"),
            P("seq", "head"),
            P("head", "seq"),
        ),
        check_vma=False,
    )
```

profile of v0, /device:TPU:109, one launch (start us, length us, event | category | flops | bytes accessed | tf_op | source)
XLA Modules:
  0.0 251.1 jit_solution(9258880873134055670)
XLA Ops:
  7.2 1.1 pad_maximum_fusion.3
  8.4 4.6 %collective-permute-start.2 = (bf16[2,1024,128]{2,1,0:T(8,128)(2,1)S(1)}, bf16[2,1024,128]{2,1,0:T(8,128)(2,1)S(1)}, u32[]{:S(2)}, u32[]{:S(2)}) collective-permute-start(bf16[2,1024,128]{2,1,0:T(8,128)(2,1)S(1)} %pad_maximum_fusion.3), channel_id=1, source_target_pairs={{0,16},{8,24},{16,32},{24,40},{32,48},{40,56},{48,64},{56,72},{64,... | collective-permute-start | bytes 1572872 | tf_op jit(solution)/shard_map/ppermute | solution.py:15
  13.0 3.5 %collective-permute-start.4 = (bf16[2,1024,128]{2,1,0:T(8,128)(2,1)S(1)}, bf16[2,1024,128]{2,1,0:T(8,128)(2,1)S(1)}, u32[]{:S(2)}, u32[]{:S(2)}) collective-permute-start(bf16[2,1024,128]{2,1,0:T(8,128)(2,1)S(1)} %pad_maximum_fusion.3), channel_id=1, source_target_pairs={{0,24},{8,32},{16,40},{24,48},{32,56},{40,64},{48,72},{56,80},{64,... | collective-permute-start | bytes 1572872 | tf_op jit(solution)/shard_map/ppermute | solution.py:15
  16.5 2.5 %collective-permute-start = (bf16[2,1024,128]{2,1,0:T(8,128)(2,1)S(1)}, bf16[2,1024,128]{2,1,0:T(8,128)(2,1)S(1)}, u32[]{:S(2)}, u32[]{:S(2)}) collective-permute-start(bf16[2,1024,128]{2,1,0:T(8,128)(2,1)S(1)} %pad_maximum_fusion.3), channel_id=1, source_target_pairs={{0,8},{8,16},{16,24},{24,32},{32,40},{40,48},{48,56},{56,64},{64,7... | collective-permute-start | bytes 1572872 | tf_op jit(solution)/shard_map/ppermute | solution.py:15
  19.0 3.0 %collective-permute-start.1 = (s32[1024]{0:T(1024)}, s32[1024]{0:T(1024)S(1)}, u32[]{:S(2)}, u32[]{:S(2)}) collective-permute-start(s32[1024]{0:T(1024)} %param.12), channel_id=1, source_target_pairs={{0,8},{8,16},{16,24},{24,32},{32,40},{40,48},{48,56},{56,64},{64,7... | collective-permute-start | bytes 12296 | tf_op jit(solution)/shard_map/ppermute | solution.py:15
  22.0 2.5 %collective-permute-start.3 = (s32[1024]{0:T(1024)}, s32[1024]{0:T(1024)S(1)}, u32[]{:S(2)}, u32[]{:S(2)}) collective-permute-start(s32[1024]{0:T(1024)} %param.12), channel_id=1, source_target_pairs={{0,16},{8,24},{16,32},{24,40},{32,48},{40,56},{48,64},{56,72},{64,... | collective-permute-start | bytes 12296 | tf_op jit(solution)/shard_map/ppermute | solution.py:15
  25.3 1.1 copy.13
  26.4 1.7 fusion.64
  28.1 2.9 %collective-permute-start.5 = (s32[1024]{0:T(1024)S(1)}, s32[1024]{0:T(1024)S(1)}, u32[]{:S(2)}, u32[]{:S(2)}) collective-permute-start(s32[1024]{0:T(1024)S(1)} %copy-done.36), channel_id=1, source_target_pairs={{0,24},{8,32},{16,40},{24,48},{32,56},{40,64},{48,72},{56,80},{64,... | collective-permute-start | bytes 12296 | tf_op jit(solution)/shard_map/ppermute | solution.py:15
  31.8 3.5 %collective-permute-done.4 = bf16[2,1024,128]{2,1,0:T(8,128)(2,1)S(1)} collective-permute-done((bf16[2,1024,128]{2,1,0:T(8,128)(2,1)S(1)}, bf16[2,1024,128]{2,1,0:T(8,128)(2,1)S(1)}, u32[]{:S(2)}, u32[]{:S(2)}) %collective-permute-start.4) | collective-permute-done | bytes 524320 | tf_op jit(solution)/shard_map/ppermute | solution.py:15
  35.9 5.8 %collective-permute-done.1 = s32[1024]{0:T(1024)S(1)} collective-permute-done((s32[1024]{0:T(1024)}, s32[1024]{0:T(1024)S(1)}, u32[]{:S(2)}, u32[]{:S(2)}) %collective-permute-start.1) | collective-permute-done | bytes 4128 | tf_op jit(solution)/shard_map/ppermute | solution.py:15
  41.8 0.8 copy-done.32
  42.6 10.4 %fusion.26 = (bf16[1024,1024]{1,0:T(8,128)(2,1)S(1)}, bf16[1024,1024]{1,0:T(8,128)(2,1)S(1)}, bf16[1024,1024]{1,0:T(8,128)(2,1)S(1)}, bf16[1024,1024]{1,0:T(8,128)(2,1)S(1)}, f32[1024,1024]{0,1:T(8,128)}) fusion(s32[1024]{0:T(1024)S(1)} %collective-permute-done.1, f32[]{:T(128)} %bitcast.295, pred[]{:T(512)S(6)} %ge.13, s32[1024]{0:T(1024)S(1)} %copy-done.36, ...), kind=kOutput, calls=%fused_computation.35 | convolution fusion | flops 312475648 | bytes 25711620 | tf_op jit(solution)/shard_map/ihd,jhd->hij/dot_general | solution.py:47
  53.1 0.8 convolution_bitcast_fusion.9
  53.9 0.8 fusion.56
  54.8 0.8 fusion.59
  55.7 0.9 fusion.63
  56.7 26.8 %all-gather.2.cloned.1.call-done = bf16[1024,1024]{1,0:T(8,128)(2,1)} async-done(((bf16[1024,128]{1,0:T(8,128)(2,1)}), bf16[1024,1024]{1,0:T(8,128)(2,1)}) %all-gather.2.cloned.1.call-update) | async-done | bytes 2097168 | tf_op jit(solution)/shard_map/all_gather | solution.py:62
  83.5 2.6 %fusion.44 = (f32[1024]{0:T(1024)S(1)}, f32[1024,128]{0,1:T(8,128)S(1)}) fusion(f32[128,1024]{1,0:T(8,128)S(1)} %get-tuple-element.20, f32[1024]{0:T(1024)S(1)} %add_rsqrt_fusion, f32[1024]{0:T(1024)S(1)} %broadcast_multiply_fusion.1, bf16[1024,128]{0,1:T(8,128)(2,1)S(1)} %copy.13, bf16[1024,1024]{1,0:T(8,128)(2,1)} %all-gather.2.cloned.1.call-done, ...), kind=kOutput, calls=%fused_computation.87 | convolution fusion | flops 269220864 | bytes 3682304 | tf_op jit(solution)/shard_map/dot_general | solution.py:63
  86.2 1.0 fusion.43
  87.2 1.8 convolution_bitcast_fusion.4
  89.0 1.7 convolution_bitcast_fusion.2
  90.7 1.7 convolution_bitcast_fusion
  92.5 1.8 fusion.51
  94.3 4.4 %fusion.32 = bf16[1024,1024]{1,0:T(8,128)(2,1)S(1)} fusion(f32[1024,1024]{0,1:T(8,128)} %get-tuple-element.18, bf16[1024,128]{0,1:T(8,128)(2,1)S(1)} %get-tuple-element.11, s32[1024]{0:T(1024)S(1)} %collective-permute-done.1, f32[]{:T(128)} %bitcast.293, pred[]{:T(512)S(6)} %ge.13, s32[1024]{0:T(1024)S(1)} %copy-done.36, bf16[2,1024,128]{2,1,0:T(8,128)(2,1)} %copy-done.32), kind=kOutput, calls=%fused_computation.41 | convolution fusion | flops 284164096 | bytes 6824449 | tf_op jit(solution)/shard_map/ihd,jhd->hij/dot_general | solution.py:91
  98.7 0.7 convolution_bitcast_fusion.5
  99.4 1.1 pad_maximum_fusion
  100.5 3.9 %collective-permute-start.6 = (f32[2,1024,128]{2,1,0:T(8,128)}, f32[2,1024,128]{2,1,0:T(8,128)}, u32[]{:S(2)}, u32[]{:S(2)}) collective-permute-start(f32[2,1024,128]{2,1,0:T(8,128)} %pad_maximum_fusion), channel_id=1, source_target_pairs={{8,0},{16,8},{24,16},{32,24},{40,32},{48,40},{56,48},{64,56},{72,6... | collective-permute-start | bytes 3145736 | tf_op jit(solution)/shard_map/ppermute | solution.py:15
  104.4 3.1 %fusion.21 = bf16[1024,1024]{1,0:T(8,128)(2,1)S(1)} fusion(f32[1024,1024]{0,1:T(8,128)S(1)} %copy-done.17, bf16[1024,128]{0,1:T(8,128)(2,1)S(1)} %get-tuple-element.11, s32[1024]{0:T(1024)S(1)} %collective-permute-done.3, f32[]{:T(128)} %bitcast.297, pred[]{:T(512)S(6)} %ge.14, s32[1024]{0:T(1024)S(1)} %copy-done.36, bf16[2,1024,128]{2,1,0:T(8,128)(2,1)S(1)} %copy-done.29), kind=kOutput, calls=%fused_computation.27 | convolution fusion | flops 284164096 | bytes 6823941 | tf_op jit(solution)/shard_map/ihd,jhd->hij/dot_general | solution.py:91
  107.5 0.7 convolution_bitcast_fusion.3
  108.3 1.1 pad_maximum_fusion.1
  109.4 3.2 %collective-permute-start.7 = (f32[2,1024,128]{2,1,0:T(8,128)}, f32[2,1024,128]{2,1,0:T(8,128)}, u32[]{:S(2)}, u32[]{:S(2)}) collective-permute-start(f32[2,1024,128]{2,1,0:T(8,128)} %pad_maximum_fusion.1), channel_id=1, source_target_pairs={{16,0},{24,8},{32,16},{40,24},{48,32},{56,40},{64,48},{72,56},{80,... | collective-permute-start | bytes 3145736 | tf_op jit(solution)/shard_map/ppermute | solution.py:15
  112.6 2.9 %fusion.10 = bf16[1024,1024]{1,0:T(8,128)(2,1)S(1)} fusion(f32[1024,1024]{0,1:T(8,128)S(1)} %copy-done.15, bf16[1024,128]{0,1:T(8,128)(2,1)S(1)} %get-tuple-element.11, s32[1024]{0:T(1024)S(1)} %collective-permute-done.5, f32[]{:T(128)} %bitcast.296, pred[]{:T(512)S(6)} %ge.15, s32[1024]{0:T(1024)S(1)} %copy-done.36, bf16[2,1024,128]{2,1,0:T(8,128)(2,1)S(1)} %copy-done.25), kind=kOutput, calls=%fused_computation.13 | convolution fusion | flops 284164096 | bytes 6823941 | tf_op jit(solution)/shard_map/ihd,jhd->hij/dot_general | solution.py:91
  115.5 0.7 convolution_bitcast_fusion.1
  116.3 1.1 pad_maximum_fusion.2
  117.4 2.4 collective-permute-start.8
  119.8 3.5 %select_convert_fusion = bf16[1024,1024]{1,0:T(8,128)(2,1)S(1)} fusion(f32[1024,1024]{1,0:T(8,128)S(1)} %copy-done.13, bf16[1024,128]{0,1:T(8,128)(2,1)S(1)} %get-tuple-element.11, bf16[1024,128]{1,0:T(8,128)(2,1)S(1)} %copy-done.31, f32[]{:T(128)} %bitcast.294, s32[1024]{0:T(1024)S(1)} %copy-done.36, pred[]{:T(512)S(6)} %ge.12), kind=kOutput, calls=%fused_computation.42 | convolution fusion | flops 286261248 | bytes 6819845 | tf_op jit(solution)/shard_map/ihd,jhd->hij/dot_general | solution.py:91
  123.4 1.5 convolution_bitcast_fusion.8
  124.9 1.0 copy.28
  125.9 2.4 fusion.57
  128.4 2.5 convolution_bitcast_fusion.7
  131.6 1.0 convolution_bitcast_fusion.6
  132.6 1.5 fusion.36
  134.1 5.0 %collective-permute-done.7 = f32[2,1024,128]{2,1,0:T(8,128)} collective-permute-done((f32[2,1024,128]{2,1,0:T(8,128)}, f32[2,1024,128]{2,1,0:T(8,128)}, u32[]{:S(2)}, u32[]{:S(2)}) %collective-permute-start.7) | collective-permute-done | bytes 1048608 | tf_op jit(solution)/shard_map/ppermute | solution.py:15
  139.2 11.9 %collective-permute-done.8 = f32[2,1024,128]{2,1,0:T(8,128)} collective-permute-done((f32[2,1024,128]{2,1,0:T(8,128)}, f32[2,1024,128]{2,1,0:T(8,128)}, u32[]{:S(2)}, u32[]{:S(2)}) %collective-permute-start.8) | collective-permute-done | bytes 1048608 | tf_op jit(solution)/shard_map/ppermute | solution.py:15
  151.1 2.1 fusion.40
  153.2 1.0 slice_bitcast_fusion
  154.2 90.0 %reduce-scatter.2.cloned.1.call-done = f32[128,32]{0,1:T(8,128)} async-done(((f32[128,1024]{0,1:T(8,128)}), f32[128,32]{0,1:T(8,128)}) %reduce-scatter.2.cloned.1.call-update) | async-done | bytes 16400 | tf_op jit(solution)/shard_map/reduce_scatter | solution.py:71
  (91 shorter events, 2.7 us)
Async XLA Ops:
  7.2 19.2 %copy-start = (bf16[1024,128]{1,0:T(8,128)(2,1)S(1)}, bf16[1024,128]{1,0:T(8,128)(2,1)}, u32[]{:S(2)}) copy-start(bf16[1024,128]{1,0:T(8,128)(2,1)} %param.8) | copy-start | bytes 786436
  7.2 20.9 %copy-start.36 = (s32[1024]{0:T(1024)S(1)}, s32[1024]{0:T(1024)}, u32[]{:S(2)}) copy-start(s32[1024]{0:T(1024)} %param.12) | copy-start | bytes 12292
  7.2 76.3 %all-gather.2.cloned.1.call-start = ((), (), s32[]{:S(2)}) async-start(), calls=%async_computation.1 | async-start | bytes 2359296 | tf_op jit(solution)/shard_map/all_gather | solution.py:62
  8.4 19.7 %collective-permute-start.2 = (bf16[2,1024,128]{2,1,0:T(8,128)(2,1)S(1)}, bf16[2,1024,128]{2,1,0:T(8,128)(2,1)S(1)}, u32[]{:S(2)}, u32[]{:S(2)}) collective-permute-start(bf16[2,1024,128]{2,1,0:T(8,128)(2,1)S(1)} %pad_maximum_fusion.3), channel_id=1, source_target_pairs={{0,16},{8,24},{16,32},{24,40},{32,48},{40,56},{48,64},{56,72},{64,... | collective-permute-start | bytes 1572872 | tf_op jit(solution)/shard_map/ppermute | solution.py:15
  13.0 22.2 %collective-permute-start.4 = (bf16[2,1024,128]{2,1,0:T(8,128)(2,1)S(1)}, bf16[2,1024,128]{2,1,0:T(8,128)(2,1)S(1)}, u32[]{:S(2)}, u32[]{:S(2)}) collective-permute-start(bf16[2,1024,128]{2,1,0:T(8,128)(2,1)S(1)} %pad_maximum_fusion.3), channel_id=1, source_target_pairs={{0,24},{8,32},{16,40},{24,48},{32,56},{40,64},{48,72},{56,80},{64,... | collective-permute-start | bytes 1572872 | tf_op jit(solution)/shard_map/ppermute | solution.py:15
  16.5 25.3 %collective-permute-start = (bf16[2,1024,128]{2,1,0:T(8,128)(2,1)S(1)}, bf16[2,1024,128]{2,1,0:T(8,128)(2,1)S(1)}, u32[]{:S(2)}, u32[]{:S(2)}) collective-permute-start(bf16[2,1024,128]{2,1,0:T(8,128)(2,1)S(1)} %pad_maximum_fusion.3), channel_id=1, source_target_pairs={{0,8},{8,16},{16,24},{24,32},{32,40},{40,48},{48,56},{56,64},{64,7... | collective-permute-start | bytes 1572872 | tf_op jit(solution)/shard_map/ppermute | solution.py:15
  19.0 22.7 %collective-permute-start.1 = (s32[1024]{0:T(1024)}, s32[1024]{0:T(1024)S(1)}, u32[]{:S(2)}, u32[]{:S(2)}) collective-permute-start(s32[1024]{0:T(1024)} %param.12), channel_id=1, source_target_pairs={{0,8},{8,16},{16,24},{24,32},{32,40},{40,48},{48,56},{56,64},{64,7... | collective-permute-start | bytes 12296 | tf_op jit(solution)/shard_map/ppermute | solution.py:15
  22.0 19.8 %collective-permute-start.3 = (s32[1024]{0:T(1024)}, s32[1024]{0:T(1024)S(1)}, u32[]{:S(2)}, u32[]{:S(2)}) collective-permute-start(s32[1024]{0:T(1024)} %param.12), channel_id=1, source_target_pairs={{0,16},{8,24},{16,32},{24,40},{32,48},{40,56},{48,64},{56,72},{64,... | collective-permute-start | bytes 12296 | tf_op jit(solution)/shard_map/ppermute | solution.py:15
  24.6 219.6 %reduce-scatter.2.cloned.1.call-start = ((), (), s32[]{:S(2)}) async-start(), calls=%async_computation.2 | async-start | bytes 540672 | tf_op jit(solution)/shard_map/reduce_scatter | solution.py:71
  28.1 14.6 %copy-start.12 = (f32[1024,1024]{1,0:T(8,128)}, f32[1024,1024]{1,0:T(8,128)S(1)}, u32[]{:S(2)}) copy-start(f32[1024,1024]{1,0:T(8,128)S(1)} %fusion.64) | copy-start | bytes 12582916
  28.1 13.7 %copy-start.27 = (bf16[2,1024,128]{2,1,0:T(8,128)(2,1)}, bf16[2,1024,128]{2,1,0:T(8,128)(2,1)S(1)}, u32[]{:S(2)}) copy-start(bf16[2,1024,128]{2,1,0:T(8,128)(2,1)S(1)} %collective-permute-done.2) | copy-start | bytes 1572868
  28.1 13.7 %collective-permute-start.5 = (s32[1024]{0:T(1024)S(1)}, s32[1024]{0:T(1024)S(1)}, u32[]{:S(2)}, u32[]{:S(2)}) collective-permute-start(s32[1024]{0:T(1024)S(1)} %copy-done.36), channel_id=1, source_target_pairs={{0,24},{8,32},{16,40},{24,48},{32,56},{40,64},{48,72},{56,80},{64,... | collective-permute-start | bytes 12296 | tf_op jit(solution)/shard_map/ppermute | solution.py:15
  31.7 21.3 %copy-start.16 = (f32[1024,1024]{0,1:T(8,128)}, f32[1024,1024]{0,1:T(8,128)S(1)}, u32[]{:S(2)}) copy-start(f32[1024,1024]{0,1:T(8,128)S(1)} %fusion.58) | copy-start | bytes 12582916
  35.2 19.5 %copy-start.24 = (bf16[2,1024,128]{2,1,0:T(8,128)(2,1)}, bf16[2,1024,128]{2,1,0:T(8,128)(2,1)S(1)}, u32[]{:S(2)}) copy-start(bf16[2,1024,128]{2,1,0:T(8,128)(2,1)S(1)} %collective-permute-done.4) | copy-start | bytes 1572868
  35.9 17.1 %copy-start.14 = (f32[1024,1024]{0,1:T(8,128)}, f32[1024,1024]{0,1:T(8,128)S(1)}, u32[]{:S(2)}) copy-start(f32[1024,1024]{0,1:T(8,128)S(1)} %fusion.61) | copy-start | bytes 12582916
  41.8 0.8 copy-start.32
  42.6 10.4 %copy-start.30 = (bf16[1024,128]{1,0:T(8,128)(2,1)S(1)}, bf16[1024,128]{1,0:T(8,128)(2,1)}, u32[]{:S(2)}) copy-start(bf16[1024,128]{1,0:T(8,128)(2,1)} %param.10) | copy-start | bytes 786436
  42.6 11.3 %copy-start.28 = (bf16[2,1024,128]{2,1,0:T(8,128)(2,1)S(1)}, bf16[2,1024,128]{2,1,0:T(8,128)(2,1)}, u32[]{:S(2)}) copy-start(bf16[2,1024,128]{2,1,0:T(8,128)(2,1)} %copy-done.27) | copy-start | bytes 1572868
  53.0 2.6 %copy-start.5 = (bf16[1024,1024]{1,0:T(8,128)(2,1)}, bf16[1024,1024]{1,0:T(8,128)(2,1)S(1)}, u32[]{:S(2)}) copy-start(bf16[1024,1024]{1,0:T(8,128)(2,1)S(1)} %get-tuple-element.16) | copy-start | bytes 6291460
  53.0 2.6 %copy-start.8 = (bf16[1024,1024]{1,0:T(8,128)(2,1)}, bf16[1024,1024]{1,0:T(8,128)(2,1)S(1)}, u32[]{:S(2)}) copy-start(bf16[1024,1024]{1,0:T(8,128)(2,1)S(1)} %get-tuple-element.17) | copy-start | bytes 6291460
  53.0 2.6 %copy-start.10 = (bf16[1024,1024]{1,0:T(8,128)(2,1)}, bf16[1024,1024]{1,0:T(8,128)(2,1)S(1)}, u32[]{:S(2)}) copy-start(bf16[1024,1024]{1,0:T(8,128)(2,1)S(1)} %get-tuple-element.15) | copy-start | bytes 6291460
  53.1 2.6 %copy-start.33 = (bf16[2,1024,128]{2,1,0:T(8,128)(2,1)S(1)}, bf16[2,1024,128]{2,1,0:T(8,128)(2,1)}, u32[]{:S(2)}) copy-start(bf16[2,1024,128]{2,1,0:T(8,128)(2,1)} %copy-done.32) | copy-start | bytes 1572868
  54.8 28.7 %copy-start.35 = (bf16[128,1024]{1,0:T(8,128)(2,1)S(1)}, bf16[128,1024]{1,0:T(8,128)(2,1)}, u32[]{:S(2)}) copy-start(bf16[128,1024]{1,0:T(8,128)(2,1)} %param.15) | copy-start | bytes 786436
  83.5 5.5 %copy-start.11 = (bf16[1024,1024]{1,0:T(8,128)(2,1)S(1)}, bf16[1024,1024]{1,0:T(8,128)(2,1)}, u32[]{:S(2)}) copy-start(bf16[1024,1024]{1,0:T(8,128)(2,1)} %copy-done.10) | copy-start | bytes 6291460
  86.1 4.6 %copy-start.9 = (bf16[1024,1024]{1,0:T(8,128)(2,1)S(1)}, bf16[1024,1024]{1,0:T(8,128)(2,1)}, u32[]{:S(2)}) copy-start(bf16[1024,1024]{1,0:T(8,128)(2,1)} %copy-done.8) | copy-start | bytes 6291460
  87.2 5.3 %copy-start.7 = (bf16[1024,1024]{1,0:T(8,128)(2,1)S(1)}, bf16[1024,1024]{1,0:T(8,128)(2,1)}, u32[]{:S(2)}) copy-start(bf16[1024,1024]{1,0:T(8,128)(2,1)} %all-gather.2.cloned.1.call-done) | copy-start | bytes 6291460
  94.2 5.2 %copy-start.23 = (f32[1,1024,128]{2,1,0:T(8,128)S(1)}, f32[1,1024,128]{2,1,0:T(8,128)}, u32[]{:S(2)}) copy-start(f32[1,1024,128]{2,1,0:T(8,128)} %convolution_bitcast_fusion.4) | copy-start | bytes 1572868
  98.6 5.7 %copy-start.17 = (f32[1024,1024]{0,1:T(8,128)S(1)}, f32[1024,1024]{0,1:T(8,128)}, u32[]{:S(2)}) copy-start(f32[1024,1024]{0,1:T(8,128)} %copy-done.16) | copy-start | bytes 12582916
  98.7 5.7 %copy-start.29 = (bf16[2,1024,128]{2,1,0:T(8,128)(2,1)S(1)}, bf16[2,1024,128]{2,1,0:T(8,128)(2,1)}, u32[]{:S(2)}) copy-start(bf16[2,1024,128]{2,1,0:T(8,128)(2,1)} %copy-done.27) | copy-start | bytes 1572868
  100.5 33.6 %collective-permute-start.6 = (f32[2,1024,128]{2,1,0:T(8,128)}, f32[2,1024,128]{2,1,0:T(8,128)}, u32[]{:S(2)}, u32[]{:S(2)}) collective-permute-start(f32[2,1024,128]{2,1,0:T(8,128)} %pad_maximum_fusion), channel_id=1, source_target_pairs={{8,0},{16,8},{24,16},{32,24},{40,32},{48,40},{56,48},{64,56},{72,6... | collective-permute-start | bytes 3145736 | tf_op jit(solution)/shard_map/ppermute | solution.py:15
  104.4 3.9 %copy-start.22 = (f32[1,1024,128]{2,1,0:T(8,128)S(1)}, f32[1,1024,128]{2,1,0:T(8,128)}, u32[]{:S(2)}) copy-start(f32[1,1024,128]{2,1,0:T(8,128)} %convolution_bitcast_fusion.2) | copy-start | bytes 1572868
  107.5 8.0 %copy-start.1 = (bf16[1024,1024]{1,0:T(8,128)(2,1)}, bf16[1024,1024]{1,0:T(8,128)(2,1)S(1)}, u32[]{:S(2)}) copy-start(bf16[1024,1024]{1,0:T(8,128)(2,1)S(1)} %fusion.21) | copy-start | bytes 6291460
  107.5 5.1 %copy-start.15 = (f32[1024,1024]{0,1:T(8,128)S(1)}, f32[1024,1024]{0,1:T(8,128)}, u32[]{:S(2)}) copy-start(f32[1024,1024]{0,1:T(8,128)} %copy-done.14) | copy-start | bytes 12582916
  107.5 5.1 %copy-start.25 = (bf16[2,1024,128]{2,1,0:T(8,128)(2,1)S(1)}, bf16[2,1024,128]{2,1,0:T(8,128)(2,1)}, u32[]{:S(2)}) copy-start(bf16[2,1024,128]{2,1,0:T(8,128)(2,1)} %copy-done.24) | copy-start | bytes 1572868
  109.4 29.8 %collective-permute-start.7 = (f32[2,1024,128]{2,1,0:T(8,128)}, f32[2,1024,128]{2,1,0:T(8,128)}, u32[]{:S(2)}, u32[]{:S(2)}) collective-permute-start(f32[2,1024,128]{2,1,0:T(8,128)} %pad_maximum_fusion.1), channel_id=1, source_target_pairs={{16,0},{24,8},{32,16},{40,24},{48,32},{56,40},{64,48},{72,56},{80,... | collective-permute-start | bytes 3145736 | tf_op jit(solution)/shard_map/ppermute | solution.py:15
  112.6 3.7 %copy-start.21 = (f32[1,1024,128]{2,1,0:T(8,128)S(1)}, f32[1,1024,128]{2,1,0:T(8,128)}, u32[]{:S(2)}) copy-start(f32[1,1024,128]{2,1,0:T(8,128)} %convolution_bitcast_fusion) | copy-start | bytes 1572868
  115.5 7.8 %copy-start.2 = (bf16[1024,1024]{1,0:T(8,128)(2,1)}, bf16[1024,1024]{1,0:T(8,128)(2,1)S(1)}, u32[]{:S(2)}) copy-start(bf16[1024,1024]{1,0:T(8,128)(2,1)S(1)} %fusion.10) | copy-start | bytes 6291460
  115.5 4.3 %copy-start.13 = (f32[1024,1024]{1,0:T(8,128)S(1)}, f32[1024,1024]{1,0:T(8,128)}, u32[]{:S(2)}) copy-start(f32[1024,1024]{1,0:T(8,128)} %copy-done.12) | copy-start | bytes 12582916
  115.5 4.3 %copy-start.31 = (bf16[1024,128]{1,0:T(8,128)(2,1)S(1)}, bf16[1024,128]{1,0:T(8,128)(2,1)}, u32[]{:S(2)}) copy-start(bf16[1024,128]{1,0:T(8,128)(2,1)} %param.10) | copy-start | bytes 786436
  117.4 33.7 %collective-permute-start.8 = (f32[2,1024,128]{2,1,0:T(8,128)}, f32[2,1024,128]{2,1,0:T(8,128)}, u32[]{:S(2)}, u32[]{:S(2)}) collective-permute-start(f32[2,1024,128]{2,1,0:T(8,128)} %pad_maximum_fusion.2), channel_id=1, source_target_pairs={{24,0},{32,8},{40,16},{48,24},{56,32},{64,40},{72,48},{80,56},{88,... | collective-permute-start | bytes 3145736 | tf_op jit(solution)/shard_map/ppermute | solution.py:15
  119.8 3.5 %copy-start.18 = (bf16[1024,128]{1,0:T(8,128)(2,1)S(1)}, bf16[1024,128]{1,0:T(8,128)(2,1)}, u32[]{:S(2)}) copy-start(bf16[1024,128]{1,0:T(8,128)(2,1)} %param.9) | copy-start | bytes 786436
  119.8 5.1 %copy-start.20 = (f32[1024,128]{0,1:T(8,128)S(1)}, f32[1024,128]{0,1:T(8,128)}, u32[]{:S(2)}) copy-start(f32[1024,128]{0,1:T(8,128)} %get-tuple-element.10) | copy-start | bytes 1572868
  123.3 1.6 copy-start.4
  125.9 5.0 %copy-start.3 = (bf16[1024,1024]{1,0:T(8,128)(2,1)S(1)}, bf16[1024,1024]{1,0:T(8,128)(2,1)}, u32[]{:S(2)}) copy-start(bf16[1024,1024]{1,0:T(8,128)(2,1)} %copy-done.2) | copy-start | bytes 6291460
  125.9 5.0 %copy-start.26 = (bf16[2,1024,128]{2,1,0:T(8,128)(2,1)S(1)}, bf16[2,1024,128]{2,1,0:T(8,128)(2,1)}, u32[]{:S(2)}) copy-start(bf16[2,1024,128]{2,1,0:T(8,128)(2,1)} %copy-done.24) | copy-start | bytes 1572868
  128.4 3.2 %copy-start.6 = (bf16[1024,1024]{1,0:T(8,128)(2,1)S(1)}, bf16[1024,1024]{1,0:T(8,128)(2,1)}, u32[]{:S(2)}) copy-start(bf16[1024,1024]{1,0:T(8,128)(2,1)} %copy-done.5) | copy-start | bytes 6291460
  128.4 4.2 %copy-start.19 = (f32[128,1024]{0,1:T(8,128)S(1)}, f32[128,1024]{0,1:T(8,128)}, u32[]{:S(2)}) copy-start(f32[128,1024]{0,1:T(8,128)} %convolution_bitcast_fusion.8) | copy-start | bytes 1572868
  128.4 4.2 %copy-start.34 = (bf16[2,1024,128]{2,1,0:T(8,128)(2,1)S(1)}, bf16[2,1024,128]{2,1,0:T(8,128)(2,1)}, u32[]{:S(2)}) copy-start(bf16[2,1024,128]{2,1,0:T(8,128)(2,1)} %copy-done.32) | copy-start | bytes 1572868
Sparse Core Ops, SparseCore 0:
  24.7 58.7 all-gather.1
  94.4 149.8 reduce-scatter.1
where the time goes:
time: 251 us
  waiting for transfers between devices  143 us (57%)
  matrix products  52.2 us (21%)
  starting transfers between devices  28.7 us (11%)
  between operations  15.4 us (6%)
  other arithmetic  7.54 us (3%)
  local copies, waits for them, and re-layouts  4.13 us (2%)
    reduce_scatter x1, waiting for transfers between devices, per_device(): lax.psum_scatter(weight_rows, 'seq', scatter_dimension=1, tiled=True)  90 us
    ppermute x9, starting transfers between devices, shifted(): return lax.ppermute(block, axis, route)  28.6 us
    all_gather x1, waiting for transfers between devices, per_device(): column_block = lax.all_gather(grad_out, 'head', axis=1, tiled=True)  26.8 us
    ppermute x9, waiting for transfers between devices, shifted(): return lax.ppermute(block, axis, route)  26.3 us
    dot_general x4, matrix products, per_device(): jnp.einsum('ihd,jhd->hij', grad_attended, v_heads, preferred_element_type...  13.9 us
    dot_general x4, matrix products, pair_scores(): jnp.einsum('ihd,jhd->hij', query_heads, k_heads, preferred_element_type=j...  13.4 us
    dot_general x4, matrix products, per_device(): jnp.einsum('hij,ihd->jhd', key_weights, grad_attended, preferred_element_...  6.23 us
    dot_general x4, matrix products, per_device(): jnp.einsum('hij,jhd->ihd', grad_scores, k_heads, preferred_element_type=j...  6.22 us
  transfers between devices with their start and end apart: 11, of which 6 were waited for; matrix products, arithmetic and copies ran while one was open for 20% of the time, Pallas kernels for 0%

commit v1 on v0

--- a/solution.py
+++ b/solution.py
@@ -59,7 +59,10 @@
     normed = centered * inv_std
     gate_heads = gates.reshape(row_count, head_count, DH).astype(jnp.float32)
     mixed = (normed * gate_heads).astype(jnp.bfloat16).reshape(row_count, feature_count)
-    column_block = lax.all_gather(grad_out, "head", axis=1, tiled=True)
+    moved = lax.axis_size("head")
+    current_value = jnp.stack([grad_out] * moved, axis=0)
+    passed = lax.all_to_all(current_value, "head", 0, 0)
+    column_block = jnp.concatenate(passed, axis=1)
     grad_mixed = lax.dot_general(
         column_block, w_out, (((1,), (1,)), ((), ())), preferred_element_type=jnp.float32
     )

time: 251 us -> 233 us (0.928); the launches traced: 251 us -> 229 us
  waiting for transfers between devices: 143 us -> 105 us
  starting transfers between devices: 28.7 us -> 46.8 us
  local copies, waits for them, and re-layouts: 4.13 us -> 8.45 us
  other arithmetic: 7.54 us -> 3.46 us
    reduce_scatter x1, waiting for transfers between devices: 90 us -> 55.1 us  [per_device(): lax.psum_scatter(weight_rows, 'seq', scatter_dimension=1, tiled=True)]
    all_gather x1 -> x0, waiting for transfers between devices: 26.8 us -> none  [per_device(): column_block = lax.all_gather(grad_out, 'head', axis=1, tiled=True)]
    ppermute x9, waiting for transfers between devices: 26.3 us -> 48 us  [shifted(): return lax.ppermute(block, axis, route)]
    ppermute x9, starting transfers between devices: 28.6 us -> 40.8 us  [shifted(): return lax.ppermute(block, axis, route)]
    all_to_all x0 -> x1, starting transfers between devices: none -> 5.97 us  [per_device(): passed = lax.all_to_all(current_value, 'head', 0, 0)]
    another operation x3, other arithmetic: 3.2 us -> 0.21 us  [per_device(): jnp.stack([keys_term.reshape(row_count, feature_count), values_term.resha...]
    unnamed x76 -> x53, local copies, waits for them, and re-layouts: 3.1 us -> 5.85 us
  transfers between devices with their start and end apart: 11 -> 11, of which waited for: 6 -> 5; matrix products, arithmetic and copies ran while one was open for 20% -> 21% of each run, Pallas kernels for 0% -> 0%
where the time goes in v1:
time: 233 us; the launch traced here: 229 us
  waiting for transfers between devices  105 us (45%)
  matrix products  50.4 us (22%)
  starting transfers between devices  46.8 us (20%)
  between operations  15.3 us (7%)
  local copies, waits for them, and re-layouts  8.45 us (4%)
  other arithmetic  3.46 us (1%)
    reduce_scatter x1, waiting for transfers between devices, per_device(): lax.psum_scatter(weight_rows, 'seq', scatter_dimension=1, tiled=True)  55.1 us
    ppermute x9, waiting for transfers between devices, shifted(): return lax.ppermute(block, axis, route)  48 us
    ppermute x9, starting transfers between devices, shifted(): return lax.ppermute(block, axis, route)  40.8 us
    dot_general x4, matrix products, per_device(): jnp.einsum('ihd,jhd->hij', grad_attended, v_heads, preferred_element_type...  16.2 us
    dot_general x4, matrix products, pair_scores(): jnp.einsum('ihd,jhd->hij', query_heads, k_heads, preferred_element_type=j...  12.7 us
    dot_general x4, matrix products, per_device(): jnp.einsum('hij,ihd->jhd', key_weights, grad_attended, preferred_element_...  6.25 us
    all_to_all x1, starting transfers between devices, per_device(): passed = lax.all_to_all(current_value, 'head', 0, 0)  5.97 us
    unnamed x53, local copies, waits for them, and re-layouts  5.85 us
  transfers between devices with their start and end apart: 11, of which 5 were waited for; matrix products, arithmetic and copies ran while one was open for 21% of the time, Pallas kernels for 0%

profile of v1, /device:TPU:109, one launch (start us, length us, event | category | flops | bytes accessed | tf_op | source)
XLA Modules:
  0.0 229.3 jit_solution(15148480760653211261)
XLA Ops:
  7.2 1.9 pad_maximum_fusion.3
  9.1 4.6 %collective-permute-start.2 = (bf16[2,1024,128]{2,1,0:T(8,128)(2,1)}, bf16[2,1024,128]{2,1,0:T(8,128)(2,1)S(1)}, u32[]{:S(2)}, u32[]{:S(2)}) collective-permute-start(bf16[2,1024,128]{2,1,0:T(8,128)(2,1)} %pad_maximum_fusion.3), channel_id=1, source_target_pairs={{0,16},{8,24},{16,32},{24,40},{32,48},{40,56},{48,64},{56,72},{64,... | collective-permute-start | bytes 1572872 | tf_op jit(solution)/shard_map/ppermute | solution.py:15
  13.8 4.0 %collective-permute-start.1 = (s32[1024]{0:T(1024)}, s32[1024]{0:T(1024)S(1)}, u32[]{:S(2)}, u32[]{:S(2)}) collective-permute-start(s32[1024]{0:T(1024)} %param.12), channel_id=1, source_target_pairs={{0,8},{8,16},{16,24},{24,32},{32,40},{40,48},{48,56},{56,64},{64,7... | collective-permute-start | bytes 12296 | tf_op jit(solution)/shard_map/ppermute | solution.py:15
  17.8 1.9 collective-permute-start.5
  19.7 2.6 %collective-permute-start.3 = (s32[1024]{0:T(1024)}, s32[1024]{0:T(1024)S(1)}, u32[]{:S(2)}, u32[]{:S(2)}) collective-permute-start(s32[1024]{0:T(1024)} %param.12), channel_id=1, source_target_pairs={{0,16},{8,24},{16,32},{24,40},{32,48},{40,56},{48,64},{56,72},{64,... | collective-permute-start | bytes 12296 | tf_op jit(solution)/shard_map/ppermute | solution.py:15
  22.4 4.4 %collective-permute-start.4 = (bf16[2,1024,128]{2,1,0:T(8,128)(2,1)}, bf16[2,1024,128]{2,1,0:T(8,128)(2,1)}, u32[]{:S(2)}, u32[]{:S(2)}) collective-permute-start(bf16[2,1024,128]{2,1,0:T(8,128)(2,1)} %pad_maximum_fusion.3), channel_id=1, source_target_pairs={{0,24},{8,32},{16,40},{24,48},{32,56},{40,64},{48,72},{56,80},{64,... | collective-permute-start | bytes 1572872 | tf_op jit(solution)/shard_map/ppermute | solution.py:15
  26.8 1.1 copy.29
  27.9 1.6 stack.32
  29.4 6.0 %all-to-all-start = ((bf16[8,1024,128]{1,2,0:T(8,128)(2,1)}), bf16[8,1024,128]{1,2,0:T(8,128)(2,1)S(1)}, u32[]{:S(2)}, u32[]{:S(2)}) async-start(bf16[8,1024,128]{1,2,0:T(8,128)(2,1)} %stack.32), calls=%async_computation | async-start | bytes 4194304 | tf_op jit(solution)/shard_map/all_to_all | solution.py:64
  36.1 1.1 copy.30
  37.9 3.3 %collective-permute-start = (bf16[2,1024,128]{2,1,0:T(8,128)(2,1)}, bf16[2,1024,128]{2,1,0:T(8,128)(2,1)S(1)}, u32[]{:S(2)}, u32[]{:S(2)}) collective-permute-start(bf16[2,1024,128]{2,1,0:T(8,128)(2,1)} %pad_maximum_fusion.3), channel_id=1, source_target_pairs={{0,8},{8,16},{16,24},{24,32},{32,40},{40,48},{48,56},{56,64},{64,7... | collective-permute-start | bytes 1572872 | tf_op jit(solution)/shard_map/ppermute | solution.py:15
  41.2 0.7 fusion.58
  42.0 1.8 fusion.61
  43.8 8.5 %collective-permute-done = bf16[2,1024,128]{2,1,0:T(8,128)(2,1)S(1)} collective-permute-done((bf16[2,1024,128]{2,1,0:T(8,128)(2,1)}, bf16[2,1024,128]{2,1,0:T(8,128)(2,1)S(1)}, u32[]{:S(2)}, u32[]{:S(2)}) %collective-permute-start) | collective-permute-done | bytes 524320 | tf_op jit(solution)/shard_map/ppermute | solution.py:15
  52.4 9.4 %fusion.26 = (bf16[1024,1024]{1,0:T(8,128)(2,1)S(1)}, bf16[1024,1024]{1,0:T(8,128)(2,1)S(1)}, bf16[1024,1024]{1,0:T(8,128)(2,1)S(1)}, bf16[1024,1024]{1,0:T(8,128)(2,1)S(1)}, f32[1024,1024]{0,1:T(8,128)}) fusion(s32[1024]{0:T(1024)S(1)} %collective-permute-done.1, f32[]{:T(128)} %bitcast.298, pred[]{:T(512)S(6)} %ge.13, s32[1024]{0:T(1024)S(1)} %copy-done.23, ...), kind=kOutput, calls=%fused_computation.35 | convolution fusion | flops 312475648 | bytes 25711620 | tf_op jit(solution)/shard_map/ihd,jhd->hij/dot_general | solution.py:47
  61.9 0.8 convolution_bitcast_fusion.9
  62.7 0.8 fusion.56
  63.5 2.0 fusion.59
  65.6 0.9 fusion.63
  66.6 1.8 all-to-all-done
  68.4 1.5 fusion.51
  69.9 1.6 fusion.44
  71.6 1.0 fusion.43
  72.6 1.7 convolution_bitcast_fusion
  74.4 1.8 convolution_bitcast_fusion.2
  76.2 1.7 convolution_bitcast_fusion.4
  78.0 5.0 %select_convert_fusion = bf16[1024,1024]{1,0:T(8,128)(2,1)S(1)} fusion(f32[1024,1024]{1,0:T(8,128)} %copy-done.9, bf16[1024,128]{0,1:T(8,128)(2,1)S(1)} %get-tuple-element.16, bf16[1024,128]{1,0:T(8,128)(2,1)} %param.10, f32[]{:T(128)} %bitcast.297, s32[1024]{0:T(1024)S(1)} %copy-done.23, pred[]{:T(512)S(6)} %ge.12), kind=kOutput, calls=%fused_computation.42 | convolution fusion | flops 286261248 | bytes 6819845 | tf_op jit(solution)/shard_map/ihd,jhd->hij/dot_general | solution.py:94
  83.0 1.0 copy.45
  84.0 4.6 %fusion.21 = bf16[1024,1024]{1,0:T(8,128)(2,1)S(1)} fusion(f32[1024,1024]{0,1:T(8,128)} %copy-done.12, bf16[1024,128]{0,1:T(8,128)(2,1)S(1)} %get-tuple-element.16, s32[1024]{0:T(1024)S(1)} %collective-permute-done.3, f32[]{:T(128)} %bitcast.300, pred[]{:T(512)S(6)} %ge.14, s32[1024]{0:T(1024)S(1)} %copy-done.23, bf16[2,1024,128]{2,1,0:T(8,128)(2,1)} %copy-done.18), kind=kOutput, calls=%fused_computation.27 | convolution fusion | flops 284164096 | bytes 6824449 | tf_op jit(solution)/shard_map/ihd,jhd->hij/dot_general | solution.py:94
  88.6 0.7 convolution_bitcast_fusion.3
  89.3 1.4 copy-done.11
  90.7 3.8 %fusion.10 = bf16[1024,1024]{1,0:T(8,128)(2,1)S(1)} fusion(f32[1024,1024]{0,1:T(8,128)S(1)} %copy-done.11, bf16[1024,128]{0,1:T(8,128)(2,1)S(1)} %get-tuple-element.16, s32[1024]{0:T(1024)S(1)} %collective-permute-done.5, f32[]{:T(128)} %bitcast.299, pred[]{:T(512)S(6)} %ge.15, s32[1024]{0:T(1024)S(1)} %copy-done.23, ...), kind=kOutput, calls=%fused_computation.13 | convolution fusion | flops 284164096 | bytes 6824449 | tf_op jit(solution)/shard_map/ihd,jhd->hij/dot_general | solution.py:94
  94.6 0.7 convolution_bitcast_fusion.1
  95.3 0.7 convolution_bitcast_fusion.8
  96.1 0.9 copy-done.24
  96.9 2.9 %fusion.32 = bf16[1024,1024]{1,0:T(8,128)(2,1)S(1)} fusion(f32[1024,1024]{0,1:T(8,128)S(1)} %copy-done.24, bf16[1024,128]{0,1:T(8,128)(2,1)S(1)} %get-tuple-element.16, s32[1024]{0:T(1024)S(1)} %collective-permute-done.1, f32[]{:T(128)} %bitcast.296, pred[]{:T(512)S(6)} %ge.13, s32[1024]{0:T(1024)S(1)} %copy-done.23, bf16[2,1024,128]{2,1,0:T(8,128)(2,1)S(1)} %copy-done.22), kind=kOutput, calls=%fused_computation.41 | convolution fusion | flops 284164096 | bytes 6823941 | tf_op jit(solution)/shard_map/ihd,jhd->hij/dot_general | solution.py:94
  99.8 0.7 convolution_bitcast_fusion.5
  100.9 14.3 %collective-permute-start.6 = (f32[2,1024,128]{2,1,0:T(8,128)S(1)}, f32[2,1024,128]{2,1,0:T(8,128)S(1)}, u32[]{:S(2)}, u32[]{:S(2)}) collective-permute-start(f32[2,1024,128]{2,1,0:T(8,128)S(1)} %pad_maximum_fusion), channel_id=1, source_target_pairs={{8,0},{16,8},{24,16},{32,24},{40,32},{48,40},{56,48},{64,56},{72,6... | collective-permute-start | bytes 3145736 | tf_op jit(solution)/shard_map/ppermute | solution.py:15
  115.3 1.9 collective-permute-start.8
  117.3 3.7 %collective-permute-start.7 = (f32[2,1024,128]{2,1,0:T(8,128)S(1)}, f32[2,1024,128]{2,1,0:T(8,128)S(1)}, u32[]{:S(2)}, u32[]{:S(2)}) collective-permute-start(f32[2,1024,128]{2,1,0:T(8,128)S(1)} %pad_maximum_fusion.1), channel_id=1, source_target_pairs={{16,0},{24,8},{32,16},{40,24},{48,32},{56,40},{64,48},{72,56},{80,... | collective-permute-start | bytes 3145736 | tf_op jit(solution)/shard_map/ppermute | solution.py:15
  121.8 0.7 convolution_bitcast_fusion.7
  122.5 1.7 fusion.60
  124.2 1.0 convolution_bitcast_fusion.6
  125.1 1.5 fusion.36
  126.7 14.8 %collective-permute-done.8 = f32[2,1024,128]{2,1,0:T(8,128)S(1)} collective-permute-done((f32[2,1024,128]{2,1,0:T(8,128)S(1)}, f32[2,1024,128]{2,1,0:T(8,128)S(1)}, u32[]{:S(2)}, u32[]{:S(2)}) %collective-permute-start.8) | collective-permute-done | bytes 1048608 | tf_op jit(solution)/shard_map/ppermute | solution.py:15
  141.5 24.6 %collective-permute-done.7 = f32[2,1024,128]{2,1,0:T(8,128)S(1)} collective-permute-done((f32[2,1024,128]{2,1,0:T(8,128)S(1)}, f32[2,1024,128]{2,1,0:T(8,128)S(1)}, u32[]{:S(2)}, u32[]{:S(2)}) %collective-permute-start.7) | collective-permute-done | bytes 1048608 | tf_op jit(solution)/shard_map/ppermute | solution.py:15
  166.3 1.0 slice_bitcast_fusion
  167.3 55.1 %reduce-scatter.2.cloned.1.call-done = f32[128,32]{0,1:T(8,128)} async-done(((f32[128,1024]{0,1:T(8,128)}), f32[128,32]{0,1:T(8,128)}) %reduce-scatter.2.cloned.1.call-update) | async-done | bytes 16400 | tf_op jit(solution)/shard_map/reduce_scatter | solution.py:74
  (68 shorter events, 2.4 us)
Async XLA Ops:
  7.2 30.0 %copy-start = (bf16[1024,128]{1,0:T(8,128)(2,1)S(1)}, bf16[1024,128]{1,0:T(8,128)(2,1)}, u32[]{:S(2)}) copy-start(bf16[1024,128]{1,0:T(8,128)(2,1)} %param.8) | copy-start | bytes 786436
  7.2 30.0 %copy-start.13 = (bf16[1024,128]{1,0:T(8,128)(2,1)S(1)}, bf16[1024,128]{1,0:T(8,128)(2,1)}, u32[]{:S(2)}) copy-start(bf16[1024,128]{1,0:T(8,128)(2,1)} %param.9) | copy-start | bytes 786436
  9.1 28.8 %collective-permute-start.2 = (bf16[2,1024,128]{2,1,0:T(8,128)(2,1)}, bf16[2,1024,128]{2,1,0:T(8,128)(2,1)S(1)}, u32[]{:S(2)}, u32[]{:S(2)}) collective-permute-start(bf16[2,1024,128]{2,1,0:T(8,128)(2,1)} %pad_maximum_fusion.3), channel_id=1, source_target_pairs={{0,16},{8,24},{16,32},{24,40},{32,48},{40,56},{48,64},{56,72},{64,... | collective-permute-start | bytes 1572872 | tf_op jit(solution)/shard_map/ppermute | solution.py:15
  13.8 30.1 %collective-permute-start.1 = (s32[1024]{0:T(1024)}, s32[1024]{0:T(1024)S(1)}, u32[]{:S(2)}, u32[]{:S(2)}) collective-permute-start(s32[1024]{0:T(1024)} %param.12), channel_id=1, source_target_pairs={{0,8},{8,16},{16,24},{24,32},{32,40},{40,48},{48,56},{56,64},{64,7... | collective-permute-start | bytes 12296 | tf_op jit(solution)/shard_map/ppermute | solution.py:15
  17.8 26.0 %collective-permute-start.5 = (s32[1024]{0:T(1024)}, s32[1024]{0:T(1024)S(1)}, u32[]{:S(2)}, u32[]{:S(2)}) collective-permute-start(s32[1024]{0:T(1024)} %param.12), channel_id=1, source_target_pairs={{0,24},{8,32},{16,40},{24,48},{32,56},{40,64},{48,72},{56,80},{64,... | collective-permute-start | bytes 12296 | tf_op jit(solution)/shard_map/ppermute | solution.py:15
  19.7 24.1 %collective-permute-start.3 = (s32[1024]{0:T(1024)}, s32[1024]{0:T(1024)S(1)}, u32[]{:S(2)}, u32[]{:S(2)}) collective-permute-start(s32[1024]{0:T(1024)} %param.12), channel_id=1, source_target_pairs={{0,16},{8,24},{16,32},{24,40},{32,48},{40,56},{48,64},{56,72},{64,... | collective-permute-start | bytes 12296 | tf_op jit(solution)/shard_map/ppermute | solution.py:15
  22.4 19.5 %collective-permute-start.4 = (bf16[2,1024,128]{2,1,0:T(8,128)(2,1)}, bf16[2,1024,128]{2,1,0:T(8,128)(2,1)}, u32[]{:S(2)}, u32[]{:S(2)}) collective-permute-start(bf16[2,1024,128]{2,1,0:T(8,128)(2,1)} %pad_maximum_fusion.3), channel_id=1, source_target_pairs={{0,24},{8,32},{16,40},{24,48},{32,56},{40,64},{48,72},{56,80},{64,... | collective-permute-start | bytes 1572872 | tf_op jit(solution)/shard_map/ppermute | solution.py:15
  29.4 38.9 %all-to-all-start = ((bf16[8,1024,128]{1,2,0:T(8,128)(2,1)}), bf16[8,1024,128]{1,2,0:T(8,128)(2,1)S(1)}, u32[]{:S(2)}, u32[]{:S(2)}) async-start(bf16[8,1024,128]{1,2,0:T(8,128)(2,1)} %stack.32), calls=%async_computation | async-start | bytes 4194304 | tf_op jit(solution)/shard_map/all_to_all | solution.py:64
  35.4 187.0 %reduce-scatter.2.cloned.1.call-start = ((), (), s32[]{:S(2)}) async-start(), calls=%async_computation.2 | async-start | bytes 540672 | tf_op jit(solution)/shard_map/reduce_scatter | solution.py:74
  37.9 14.5 %copy-start.9 = (f32[1024,1024]{1,0:T(8,128)}, f32[1024,1024]{1,0:T(8,128)S(1)}, u32[]{:S(2)}) copy-start(f32[1024,1024]{1,0:T(8,128)S(1)} %fusion.64) | copy-start | bytes 12582916
  37.9 14.5 %copy-start.23 = (s32[1024]{0:T(1024)S(1)}, s32[1024]{0:T(1024)}, u32[]{:S(2)}) copy-start(s32[1024]{0:T(1024)} %param.12) | copy-start | bytes 12292
  37.9 24.8 %copy-start.18 = (bf16[2,1024,128]{2,1,0:T(8,128)(2,1)}, bf16[2,1024,128]{2,1,0:T(8,128)(2,1)S(1)}, u32[]{:S(2)}) copy-start(bf16[2,1024,128]{2,1,0:T(8,128)(2,1)S(1)} %collective-permute-done.2) | copy-start | bytes 1572868
  37.9 14.4 %collective-permute-start = (bf16[2,1024,128]{2,1,0:T(8,128)(2,1)}, bf16[2,1024,128]{2,1,0:T(8,128)(2,1)S(1)}, u32[]{:S(2)}, u32[]{:S(2)}) collective-permute-start(bf16[2,1024,128]{2,1,0:T(8,128)(2,1)} %pad_maximum_fusion.3), channel_id=1, source_target_pairs={{0,8},{8,16},{16,24},{24,32},{32,40},{40,48},{48,56},{56,64},{64,7... | collective-permute-start | bytes 1572872 | tf_op jit(solution)/shard_map/ppermute | solution.py:15
  41.9 19.9 %copy-start.12 = (f32[1024,1024]{0,1:T(8,128)}, f32[1024,1024]{0,1:T(8,128)S(1)}, u32[]{:S(2)}) copy-start(f32[1024,1024]{0,1:T(8,128)S(1)} %fusion.58) | copy-start | bytes 12582916
  43.8 18.0 %copy-start.10 = (f32[1024,1024]{0,1:T(8,128)}, f32[1024,1024]{0,1:T(8,128)S(1)}, u32[]{:S(2)}) copy-start(f32[1024,1024]{0,1:T(8,128)S(1)} %fusion.61) | copy-start | bytes 12582916
  52.4 13.2 %copy-start.21 = (bf16[2,1024,128]{2,1,0:T(8,128)(2,1)}, bf16[2,1024,128]{2,1,0:T(8,128)(2,1)S(1)}, u32[]{:S(2)}) copy-start(bf16[2,1024,128]{2,1,0:T(8,128)(2,1)S(1)} %collective-permute-done) | copy-start | bytes 1572868
  52.4 9.5 %copy-start.20 = (bf16[1024,128]{1,0:T(8,128)(2,1)S(1)}, bf16[1024,128]{1,0:T(8,128)(2,1)}, u32[]{:S(2)}) copy-start(bf16[1024,128]{1,0:T(8,128)(2,1)} %param.10) | copy-start | bytes 786436
  61.8 3.7 %copy-start.3 = (bf16[1024,1024]{1,0:T(8,128)(2,1)}, bf16[1024,1024]{1,0:T(8,128)(2,1)S(1)}, u32[]{:S(2)}) copy-start(bf16[1024,1024]{1,0:T(8,128)(2,1)S(1)} %get-tuple-element.21) | copy-start | bytes 6291460
  61.8 3.7 %copy-start.5 = (bf16[1024,1024]{1,0:T(8,128)(2,1)}, bf16[1024,1024]{1,0:T(8,128)(2,1)S(1)}, u32[]{:S(2)}) copy-start(bf16[1024,1024]{1,0:T(8,128)(2,1)S(1)} %get-tuple-element.20) | copy-start | bytes 6291460
  61.8 3.7 %copy-start.7 = (bf16[1024,1024]{1,0:T(8,128)(2,1)}, bf16[1024,1024]{1,0:T(8,128)(2,1)S(1)}, u32[]{:S(2)}) copy-start(bf16[1024,1024]{1,0:T(8,128)(2,1)S(1)} %get-tuple-element.22) | copy-start | bytes 6291460
  61.8 3.7 %copy-start.1 = (bf16[1024,1024]{1,0:T(8,128)(2,1)}, bf16[1024,1024]{1,0:T(8,128)(2,1)S(1)}, u32[]{:S(2)}) copy-start(bf16[1024,1024]{1,0:T(8,128)(2,1)S(1)} %get-tuple-element.19) | copy-start | bytes 6291460
  69.9 2.7 %copy-start.8 = (bf16[1024,1024]{1,0:T(8,128)(2,1)S(1)}, bf16[1024,1024]{1,0:T(8,128)(2,1)}, u32[]{:S(2)}) copy-start(bf16[1024,1024]{1,0:T(8,128)(2,1)} %copy-done.7) | copy-start | bytes 6291460
  69.9 4.4 %copy-start.6 = (bf16[1024,1024]{1,0:T(8,128)(2,1)S(1)}, bf16[1024,1024]{1,0:T(8,128)(2,1)}, u32[]{:S(2)}) copy-start(bf16[1024,1024]{1,0:T(8,128)(2,1)} %copy-done.5) | copy-start | bytes 6291460
  71.5 4.6 %copy-start.2 = (bf16[1024,1024]{1,0:T(8,128)(2,1)S(1)}, bf16[1024,1024]{1,0:T(8,128)(2,1)}, u32[]{:S(2)}) copy-start(bf16[1024,1024]{1,0:T(8,128)(2,1)} %copy-done.1) | copy-start | bytes 6291460
  77.9 5.0 %copy-start.14 = (f32[1024,128]{0,1:T(8,128)S(1)}, f32[1024,128]{0,1:T(8,128)}, u32[]{:S(2)}) copy-start(f32[1024,128]{0,1:T(8,128)} %get-tuple-element.15) | copy-start | bytes 1572868
  88.6 2.2 copy-start.11
  94.6 1.5 copy-start.22
  94.6 2.3 %copy-start.24 = (f32[1024,1024]{0,1:T(8,128)S(1)}, f32[1024,1024]{0,1:T(8,128)}, u32[]{:S(2)}) copy-start(f32[1024,1024]{0,1:T(8,128)} %get-tuple-element.23) | copy-start | bytes 12582916
  99.8 1.0 copy-start.17
  99.8 15.4 %copy-start.16 = (f32[1,1024,128]{2,1,0:T(8,128)S(1)}, f32[1,1024,128]{2,1,0:T(8,128)}, u32[]{:S(2)}) copy-start(f32[1,1024,128]{2,1,0:T(8,128)} %convolution_bitcast_fusion) | copy-start | bytes 1572868
  99.8 17.4 %copy-start.15 = (f32[1,1024,128]{2,1,0:T(8,128)S(1)}, f32[1,1024,128]{2,1,0:T(8,128)}, u32[]{:S(2)}) copy-start(f32[1,1024,128]{2,1,0:T(8,128)} %convolution_bitcast_fusion.2) | copy-start | bytes 1572868
  100.8 20.2 %copy-start.19 = (bf16[2,1024,128]{2,1,0:T(8,128)(2,1)S(1)}, bf16[2,1024,128]{2,1,0:T(8,128)(2,1)}, u32[]{:S(2)}) copy-start(bf16[2,1024,128]{2,1,0:T(8,128)(2,1)} %copy-done.18) | copy-start | bytes 1572868
  100.9 25.7 %collective-permute-start.6 = (f32[2,1024,128]{2,1,0:T(8,128)S(1)}, f32[2,1024,128]{2,1,0:T(8,128)S(1)}, u32[]{:S(2)}, u32[]{:S(2)}) collective-permute-start(f32[2,1024,128]{2,1,0:T(8,128)S(1)} %pad_maximum_fusion), channel_id=1, source_target_pairs={{8,0},{16,8},{24,16},{32,24},{40,32},{48,40},{56,48},{64,56},{72,6... | collective-permute-start | bytes 3145736 | tf_op jit(solution)/shard_map/ppermute | solution.py:15
  115.3 26.2 %collective-permute-start.8 = (f32[2,1024,128]{2,1,0:T(8,128)S(1)}, f32[2,1024,128]{2,1,0:T(8,128)S(1)}, u32[]{:S(2)}, u32[]{:S(2)}) collective-permute-start(f32[2,1024,128]{2,1,0:T(8,128)S(1)} %pad_maximum_fusion.2), channel_id=1, source_target_pairs={{24,0},{32,8},{40,16},{48,24},{56,32},{64,40},{72,48},{80,56},{88,... | collective-permute-start | bytes 3145736 | tf_op jit(solution)/shard_map/ppermute | solution.py:15
  117.3 48.8 %collective-permute-start.7 = (f32[2,1024,128]{2,1,0:T(8,128)S(1)}, f32[2,1024,128]{2,1,0:T(8,128)S(1)}, u32[]{:S(2)}, u32[]{:S(2)}) collective-permute-start(f32[2,1024,128]{2,1,0:T(8,128)S(1)} %pad_maximum_fusion.1), channel_id=1, source_target_pairs={{16,0},{24,8},{32,16},{40,24},{48,32},{56,40},{64,48},{72,56},{80,... | collective-permute-start | bytes 3145736 | tf_op jit(solution)/shard_map/ppermute | solution.py:15
  121.8 2.4 %copy-start.4 = (bf16[1024,1024]{1,0:T(8,128)(2,1)S(1)}, bf16[1024,1024]{1,0:T(8,128)(2,1)}, u32[]{:S(2)}) copy-start(bf16[1024,1024]{1,0:T(8,128)(2,1)} %copy-done.3) | copy-start | bytes 6291460
Sparse Core Ops, SparseCore 0:
  78.1 144.3 reduce-scatter.1
